TPU v7x, 256 devices: a whole 4x4x8 slice. The times are simulated.
256 devices in a mesh: dp: 32 (over y, z_hi, core), tensor: 8 (over z_lo, x).
Axes of the slice: x: 4, y: 4, z: 8 (z_hi: 4, z_lo: 2; z = z_hi * 2 + z_lo), core: 2. Of those that a mesh axis runs over, the one named last changes fastest.
Arguments:
- inputs: bfloat16 [32768, 2048], P(('dp', 'tensor')), may hold values from -6 to 6
- norm_gain: float32 [2048], replicated, may hold values from 0.1 to 1.9
- proj_weight: bfloat16 [2048, 3, 2048], P('dp', None, 'tensor'), may hold values from -0.125 to 0.125
- filters: float32 [3, 7, 2048], P(None, None, 'tensor'), may hold values from -2.4 to 2.4
- cotangent: bfloat16 [32768, 2048], P('dp', 'tensor'), may hold values from -18 to 18
Outputs:
- mixed: bfloat16 [32768, 2048], P('dp', 'tensor')
- grad_inputs: bfloat16 [32768, 2048], P(('dp', 'tensor'))
- grad_proj: bfloat16 [2048, 3, 2048], P('dp', None, 'tensor')
- grad_filters: float32 [3, 7, 2048], P(None, None, 'tensor')
- grad_gain: float32 [2048], replicated
All inputs are finite; a program needn't handle non-finite values.
Results may differ from a plain program's by a relative error of at most 0.02.
Values may be sent and summed in bfloat16 or wider, within the bound.
No kernel may reach another device: no remote copies, remote signals or barrier semaphores. Data moves between devices by JAX's collectives and lax.ppermute only.
A program may use at most 64 MiB of HBM per device.

v0:
```python
import jax
import jax.numpy as jnp
from jax import lax
from jax.sharding import PartitionSpec as P


def passed_along(shard, axis, by):
    size = lax.axis_size(axis)
    pairs = [(i, i + by) for i in range(size) if 0 <= i + by < size]
    return lax.ppermute(shard, axis, pairs)


def body(inputs, norm_gain, proj_weight, filters, cotangent):
    taps = filters.shape[1]
    width = taps - 1
    wide = inputs.astype(jnp.float32)
    inv_rms = lax.rsqrt(jnp.mean(wide * wide, axis=1, keepdims=True) + 1e-05)
    normed = (wide * inv_rms * norm_gain).astype(jnp.bfloat16)
    weights = lax.all_gather(proj_weight, "dp", axis=0, tiled=True)
    positions = lax.all_gather(normed, "tensor", axis=0, tiled=True)
    length = positions.shape[0]
    streams = jnp.einsum(
        "td,dsc->tsc", positions, weights, preferred_element_type=jnp.float32
    ).astype(jnp.bfloat16)
    before = passed_along(streams[length - width :], "dp", 1)
    extended = jnp.concatenate([before, streams], axis=0).astype(jnp.float32)
    conv = jnp.zeros(streams.shape, jnp.float32)
    for tap in range(taps):
        conv = conv + filters[:, tap, :] * extended[width - tap : width - tap + length]
    mixed = (conv[:, 0] * conv[:, 1] * conv[:, 2]).astype(jnp.bfloat16)
    grad_out = cotangent.astype(jnp.float32)
    grad_conv = jnp.stack(
        [
            grad_out * conv[:, 1] * conv[:, 2],
            grad_out * conv[:, 0] * conv[:, 2],
            grad_out * conv[:, 0] * conv[:, 1],
        ],
        axis=1,
    )
    after = passed_along(grad_conv[:width], "dp", -1)
    grad_extended = jnp.concatenate([grad_conv, after], axis=0)
    grad_acc = jnp.zeros(streams.shape, jnp.float32)
    for tap in range(taps):
        grad_acc = grad_acc + filters[:, tap, :] * grad_extended[tap : tap + length]
    grad_streams = grad_acc.astype(jnp.bfloat16)
    filter_local = jnp.stack(
        [
            jnp.sum(grad_conv * extended[width - tap : width - tap + length], axis=0)
            for tap in range(taps)
        ],
        axis=1,
    )
    normed_terms = jnp.einsum(
        "tsc,dsc->td", grad_streams, weights, preferred_element_type=jnp.float32
    )
    grad_normed = lax.psum_scatter(
        normed_terms.astype(jnp.bfloat16), "tensor", scatter_dimension=0, tiled=True
    ).astype(jnp.float32)
    weight_terms = jnp.einsum(
        "td,tsc->dsc", positions, grad_streams, preferred_element_type=jnp.float32
    )
    grad_proj = lax.psum_scatter(
        weight_terms.astype(jnp.bfloat16), "dp", scatter_dimension=0, tiled=True
    )
    scaled = norm_gain * grad_normed
    grad_inputs = inv_rms * (
        scaled - wide * inv_rms * inv_rms * jnp.mean(scaled * wide, axis=1, keepdims=True)
    )
    gain_local = jnp.sum(grad_normed * wide * inv_rms, axis=0)
    grad_filters = lax.psum(filter_local, "dp")
    grad_gain = lax.psum(gain_local, ("dp", "tensor"))
    return (mixed, grad_inputs.astype(jnp.bfloat16), grad_proj, grad_filters, grad_gain)


def solution(mesh):
    return jax.shard_map(
        body,
        mesh=mesh,
        in_specs=(
            P(("dp", "tensor"), None),
            P(),
            P("dp", None, "tensor"),
            P(None, None, "tensor"),
            P("dp", "tensor"),
        ),
        out_specs=(
            P("dp", "tensor"),
            P(("dp", "tensor"), None),
            P("dp", None, "tensor"),
            P(None, None, "tensor"),
            P(),
        ),
        check_vma=False,
    )
```

profile of v0, /device:TPU:1, one launch (start us, length us, event | category | flops | bytes accessed | tf_op | source)
XLA Modules:
  0.0 393.9 jit_solution(4973453960555978686)
XLA Ops:
  7.2 0.0 all-gather.5.cloned.1.call-start
  7.2 0.7 all-gather.5.cloned.1.call-update
  7.9 0.0 all-gather.3.cloned.1.call-start
  7.9 1.2 fusion.26
  9.2 2.0 fusion.20
  11.2 0.0 all-gather.3.cloned.1.call-update
  11.2 0.0 reduce-scatter.3.cloned.1.call-start
  11.3 1.0 fusion.30
  12.3 59.7 %all-gather.5.cloned.1.call-done = bf16[2048,3,256]{2,0,1:T(8,128)(2,1)} async-done(((bf16[64,3,256]{2,0,1:T(8,128)(2,1)}), bf16[2048,3,256]{2,0,1:T(8,128)(2,1)}) %all-gather.5.cloned.1.call-update) | async-done | bytes 3145744 | tf_op jit(solution)/shard_map/all_gather | solution.py:19
  72.0 54.9 %all-gather.3.cloned.1.call-done = bf16[1024,2048]{1,0:T(8,128)(2,1)} async-done(((bf16[128,2048]{1,0:T(8,128)(2,1)}), bf16[1024,2048]{1,0:T(8,128)(2,1)}) %all-gather.3.cloned.1.call-update) | async-done | bytes 4194320 | tf_op jit(solution)/shard_map/all_gather | solution.py:20
  126.9 6.6 %fusion.14 = bf16[1024,3,256]{2,0,1:T(8,128)(2,1)S(1)} fusion(bf16[2048,3,256]{2,0,1:T(8,128)(2,1)} %all-gather.5.cloned.1.call-done, bf16[1024,2048]{1,0:T(8,128)(2,1)} %all-gather.3.cloned.1.call-done), kind=kOutput, calls=%fused_computation.33 | convolution fusion | flops 3222011904 | bytes 8912896 | tf_op jit(solution)/shard_map/td,dsc->tsc/dot_general | solution.py:22
  133.5 4.7 %collective-permute-start = (bf16[6,3,256]{2,0,1:T(8,128)(2,1)S(1)}, bf16[6,3,256]{2,0,1:T(8,128)(2,1)S(1)}, u32[]{:S(2)}, u32[]{:S(2)}) collective-permute-start(bf16[6,3,256]{2,0,1:T(8,128)(2,1)S(1)} %slice.120), channel_id=1, source_target_pairs={{0,8},{8,16},{16,24},{24,32},{32,40},{40,48},{48,56},{56,64},{64,7... | collective-permute-start | bytes 27656 | tf_op jit(solution)/shard_map/ppermute | solution.py:10
  138.3 0.8 collective-permute-done
  139.1 0.3 maximum_convert_fusion
  139.4 0.0 copy-start.1
  139.4 2.6 multiply_add_fusion
  142.0 1.2 fusion.25
  143.2 2.9 multiply_reduce_fusion
  146.0 1.9 collective-permute-start.1
  148.0 4.8 %collective-permute-done.1 = f32[6,3,256]{2,0,1:T(8,128)S(1)} collective-permute-done((f32[6,3,256]{2,0,1:T(8,128)S(1)}, f32[6,3,256]{2,0,1:T(8,128)S(1)}, u32[]{:S(2)}, u32[]{:S(2)}) %collective-permute-start.1) | collective-permute-done | bytes 18464 | tf_op jit(solution)/shard_map/ppermute | solution.py:10
  152.8 0.2 pad_maximum_fusion
  153.0 2.7 fusion.8
  155.8 5.1 %bitcast_convert_fusion = bf16[1024,2048]{1,0:T(8,128)(2,1)} fusion(bf16[1024,3,256]{2,0,1:T(8,128)(2,1)S(1)} %fusion.8, bf16[2048,3,256]{2,0,1:T(8,128)(2,1)S(1)} %copy-done.3), kind=kOutput, calls=%fused_computation | convolution fusion | flops 3223322624 | bytes 8912896 | tf_op jit(solution)/shard_map/tsc,dsc->td/dot_general | solution.py:53
  160.8 0.0 reduce-scatter.3.cloned.1.call-update
  160.9 0.2 reduce-scatter.5.cloned.1.call-start
  161.1 7.5 %fusion.4 = bf16[2048,3,256]{2,0,1:T(8,128)(2,1)} fusion(bf16[1024,3,256]{2,0,1:T(8,128)(2,1)S(1)} %fusion.8, bf16[1024,2048]{1,0:T(8,128)(2,1)} %all-gather.3.cloned.1.call-done), kind=kOutput, calls=%fused_computation.5 | convolution fusion | flops 3222798336 | bytes 8912896 | tf_op jit(solution)/shard_map/td,tsc->dsc/dot_general | solution.py:59
  168.6 0.0 reduce-scatter.5.cloned.1.call-update
  168.7 135.1 %psum.14 = f32[3,7,256]{2,0,1:T(4,128)S(1)} all-reduce(f32[3,7,256]{2,0,1:T(4,128)S(1)} %constant_dynamic-update-slice_fusion), channel_id=1, replica_groups=mesh['dp'=32,'tensor'=8] {'dp'}, use_global_device_ids=true, to_apply=%region_11.0 | all-reduce | flops 5376 | bytes 43008 | tf_op jit(solution)/shard_map/psum | solution.py:70
  303.8 0.6 copy.12
  304.5 1.4 fusion.29
  305.8 79.3 %psum.15 = f32[2048]{0:T(1024)} all-reduce(f32[2048]{0:T(1024)S(1)} %get-tuple-element.17), channel_id=1, replica_groups=mesh['dp'=32,'tensor'=8] {'dp','tensor'}, use_global_device_ids=true, to_apply=%region_13.0 | all-reduce | flops 2048 | bytes 16384 | tf_op jit(solution)/shard_map/psum | solution.py:71
  385.2 2.2 fusion.23
  (24 shorter events, 0.1 us)
Async XLA Ops:
  7.2 64.9 %all-gather.5.cloned.1.call-start = ((), (), s32[]{:S(2)}) async-start(), calls=%async_computation.3 | async-start | bytes 3244032 | tf_op jit(solution)/shard_map/all_gather | solution.py:19
  7.9 119.0 %all-gather.3.cloned.1.call-start = ((), (), s32[]{:S(2)}) async-start(), calls=%async_computation.2 | async-start | bytes 4718592 | tf_op jit(solution)/shard_map/all_gather | solution.py:20
  11.2 293.2 %reduce-scatter.3.cloned.1.call-start = ((), (), s32[]{:S(2)}) async-start(), calls=%async_computation.4 | async-start | bytes 4718592 | tf_op jit(solution)/shard_map/reduce_scatter | solution.py:56
  133.5 5.5 %collective-permute-start = (bf16[6,3,256]{2,0,1:T(8,128)(2,1)S(1)}, bf16[6,3,256]{2,0,1:T(8,128)(2,1)S(1)}, u32[]{:S(2)}, u32[]{:S(2)}) collective-permute-start(bf16[6,3,256]{2,0,1:T(8,128)(2,1)S(1)} %slice.120), channel_id=1, source_target_pairs={{0,8},{8,16},{16,24},{24,32},{32,40},{40,48},{48,56},{56,64},{64,7... | collective-permute-start | bytes 27656 | tf_op jit(solution)/shard_map/ppermute | solution.py:10
  139.4 2.6 copy-start.1
  146.0 6.8 %collective-permute-start.1 = (f32[6,3,256]{2,0,1:T(8,128)S(1)}, f32[6,3,256]{2,0,1:T(8,128)S(1)}, u32[]{:S(2)}, u32[]{:S(2)}) collective-permute-start(f32[6,3,256]{2,0,1:T(8,128)S(1)} %slice.131), channel_id=1, source_target_pairs={{8,0},{16,8},{24,16},{32,24},{40,32},{48,40},{56,48},{64,56},{72,6... | collective-permute-start | bytes 55304 | tf_op jit(solution)/shard_map/ppermute | solution.py:10
  153.0 2.7 copy-start.3
  160.9 226.5 %reduce-scatter.5.cloned.1.call-start = ((), (), s32[]{:S(2)}) async-start(), calls=%async_computation.5 | async-start | bytes 3244032 | tf_op jit(solution)/shard_map/reduce_scatter | solution.py:62
  168.6 135.8 %copy-start = (bf16[128,2048]{1,0:T(8,128)(2,1)S(1)}, bf16[128,2048]{1,0:T(8,128)(2,1)}, u32[]{:S(2)}) copy-start(bf16[128,2048]{1,0:T(8,128)(2,1)} %param.5) | copy-start | bytes 1572868
  168.6 135.8 %copy-start.2 = (f32[2048]{0:T(1024)S(1)}, f32[2048]{0:T(1024)}, u32[]{:S(2)}) copy-start(f32[2048]{0:T(1024)} %param.6) | copy-start | bytes 24580
Sparse Core Ops, SparseCore 0:
  10.7 61.3 all-gather.4
  74.4 52.5 all-gather.2
  161.0 54.1 reduce-scatter.2
  219.5 92.7 reduce-scatter.4
where the time goes:
time: 394 us
  blocking collectives  214 us (54%)
  waiting for transfers between devices  121 us (31%)
  matrix products  19.2 us (5%)
  other arithmetic  16.6 us (4%)
  between operations  13.9 us (4%)
  starting transfers between devices  6.99 us (2%)
    psum x1, blocking collectives, body(): grad_filters = lax.psum(filter_local, 'dp')  135 us
    psum x1, blocking collectives, body(): grad_gain = lax.psum(gain_local, ('dp', 'tensor'))  79.3 us
    all_gather x1, waiting for transfers between devices, body(): weights = lax.all_gather(proj_weight, 'dp', axis=0, tiled=True)  59.7 us
    all_gather x1, waiting for transfers between devices, body(): positions = lax.all_gather(normed, 'tensor', axis=0, tiled=True)  54.9 us
  transfers between devices with their start and end apart: 6, of which 4 were waited for; matrix products, arithmetic and copies ran while one was open for 4% of the time, Pallas kernels for 0%

commit v1 on v0

--- a/solution.py
+++ b/solution.py
@@ -68,7 +68,8 @@
     )
     gain_local = jnp.sum(grad_normed * wide * inv_rms, axis=0)
     grad_filters = lax.psum(filter_local, "dp")
-    grad_gain = lax.psum(gain_local, ("dp", "tensor"))
+    answer = lax.psum(gain_local, "tensor")
+    grad_gain = lax.psum(answer, "dp")
     return (mixed, grad_inputs.astype(jnp.bfloat16), grad_proj, grad_filters, grad_gain)
 
 

time: 394 us -> 382 us (0.970); the launches traced: 394 us -> 376 us
  blocking collectives: 214 us -> 151 us
  waiting for transfers between devices: 121 us -> 167 us
    psum x1, blocking collectives: 79.3 us -> 13.4 us  [body(): answer = lax.psum(gain_local, 'tensor')]
    reduce_scatter x1, waiting for transfers between devices: 0.01 us -> 45.6 us  [body(): lax.psum_scatter(normed_terms.astype(jnp.bfloat16), 'tensor', scatter_dim...]
  transfers between devices with their start and end apart: 6 -> 6, of which waited for: 4 -> 5; matrix products, arithmetic and copies ran while one was open for 4% -> 4% of each run, Pallas kernels for 0% -> 0%
where the time goes in v1:
time: 382 us; the launch traced here: 376 us
  waiting for transfers between devices  167 us (44%)
  blocking collectives  151 us (40%)
  matrix products  19.2 us (5%)
  other arithmetic  16.6 us (4%)
  between operations  13.9 us (4%)
  starting transfers between devices  6.99 us (2%)
    psum x1, blocking collectives, body(): grad_filters = lax.psum(filter_local, 'dp')  138 us
    all_gather x1, waiting for transfers between devices, body(): weights = lax.all_gather(proj_weight, 'dp', axis=0, tiled=True)  59.7 us
    all_gather x1, waiting for transfers between devices, body(): positions = lax.all_gather(normed, 'tensor', axis=0, tiled=True)  54.9 us
    reduce_scatter x1, waiting for transfers between devices, body(): lax.psum_scatter(normed_terms.astype(jnp.bfloat16), 'tensor', scatter_dim...  45.6 us
    psum x1, blocking collectives, body(): answer = lax.psum(gain_local, 'tensor')  13.4 us
  transfers between devices with their start and end apart: 6, of which 5 were waited for; matrix products, arithmetic and copies ran while one was open for 4% of the time, Pallas kernels for 0%

profile of v1, /device:TPU:1, one launch (start us, length us, event | category | flops | bytes accessed | tf_op | source)
XLA Modules:
  0.0 376.2 jit_solution(13106994097221643583)
XLA Ops:
  7.2 0.0 all-gather.5.cloned.1.call-start
  7.2 0.7 all-gather.5.cloned.1.call-update
  7.9 0.0 all-gather.3.cloned.1.call-start
  7.9 1.2 fusion.26
  9.2 2.0 fusion.20
  11.2 0.0 all-gather.3.cloned.1.call-update
  11.2 0.0 reduce-scatter.3.cloned.1.call-start
  11.3 1.0 fusion.30
  12.3 59.7 %all-gather.5.cloned.1.call-done = bf16[2048,3,256]{2,0,1:T(8,128)(2,1)} async-done(((bf16[64,3,256]{2,0,1:T(8,128)(2,1)}), bf16[2048,3,256]{2,0,1:T(8,128)(2,1)}) %all-gather.5.cloned.1.call-update) | async-done | bytes 3145744 | tf_op jit(solution)/shard_map/all_gather | solution.py:19
  72.0 54.9 %all-gather.3.cloned.1.call-done = bf16[1024,2048]{1,0:T(8,128)(2,1)} async-done(((bf16[128,2048]{1,0:T(8,128)(2,1)}), bf16[1024,2048]{1,0:T(8,128)(2,1)}) %all-gather.3.cloned.1.call-update) | async-done | bytes 4194320 | tf_op jit(solution)/shard_map/all_gather | solution.py:20
  126.9 6.6 %fusion.14 = bf16[1024,3,256]{2,0,1:T(8,128)(2,1)S(1)} fusion(bf16[2048,3,256]{2,0,1:T(8,128)(2,1)} %all-gather.5.cloned.1.call-done, bf16[1024,2048]{1,0:T(8,128)(2,1)} %all-gather.3.cloned.1.call-done), kind=kOutput, calls=%fused_computation.33 | convolution fusion | flops 3222011904 | bytes 8912896 | tf_op jit(solution)/shard_map/td,dsc->tsc/dot_general | solution.py:22
  133.5 4.7 %collective-permute-start = (bf16[6,3,256]{2,0,1:T(8,128)(2,1)S(1)}, bf16[6,3,256]{2,0,1:T(8,128)(2,1)S(1)}, u32[]{:S(2)}, u32[]{:S(2)}) collective-permute-start(bf16[6,3,256]{2,0,1:T(8,128)(2,1)S(1)} %slice.120), channel_id=1, source_target_pairs={{0,8},{8,16},{16,24},{24,32},{32,40},{40,48},{48,56},{56,64},{64,7... | collective-permute-start | bytes 27656 | tf_op jit(solution)/shard_map/ppermute | solution.py:10
  138.3 0.8 collective-permute-done
  139.1 0.3 maximum_convert_fusion
  139.4 2.6 multiply_add_fusion
  142.0 1.2 fusion.25
  143.2 2.9 multiply_reduce_fusion
  146.0 1.9 collective-permute-start.1
  148.0 4.8 %collective-permute-done.1 = f32[6,3,256]{2,0,1:T(8,128)S(1)} collective-permute-done((f32[6,3,256]{2,0,1:T(8,128)S(1)}, f32[6,3,256]{2,0,1:T(8,128)S(1)}, u32[]{:S(2)}, u32[]{:S(2)}) %collective-permute-start.1) | collective-permute-done | bytes 18464 | tf_op jit(solution)/shard_map/ppermute | solution.py:10
  152.8 0.2 pad_maximum_fusion
  153.0 2.7 fusion.8
  155.8 5.1 %bitcast_convert_fusion = bf16[1024,2048]{1,0:T(8,128)(2,1)} fusion(bf16[1024,3,256]{2,0,1:T(8,128)(2,1)S(1)} %fusion.8, bf16[2048,3,256]{2,0,1:T(8,128)(2,1)S(1)} %copy-done.3), kind=kOutput, calls=%fused_computation | convolution fusion | flops 3223322624 | bytes 8912896 | tf_op jit(solution)/shard_map/tsc,dsc->td/dot_general | solution.py:53
  160.8 0.0 reduce-scatter.3.cloned.1.call-update
  160.9 0.2 reduce-scatter.5.cloned.1.call-start
  161.1 7.5 %fusion.4 = bf16[2048,3,256]{2,0,1:T(8,128)(2,1)} fusion(bf16[1024,3,256]{2,0,1:T(8,128)(2,1)S(1)} %fusion.8, bf16[1024,2048]{1,0:T(8,128)(2,1)} %all-gather.3.cloned.1.call-done), kind=kOutput, calls=%fused_computation.5 | convolution fusion | flops 3222798336 | bytes 8912896 | tf_op jit(solution)/shard_map/td,tsc->dsc/dot_general | solution.py:59
  168.6 0.0 reduce-scatter.5.cloned.1.call-update
  168.7 45.6 %reduce-scatter.3.cloned.1.call-done = bf16[128,2048]{1,0:T(8,128)(2,1)} async-done(((bf16[1024,2048]{1,0:T(8,128)(2,1)}), bf16[128,2048]{1,0:T(8,128)(2,1)}) %reduce-scatter.3.cloned.1.call-update) | async-done | bytes 524304 | tf_op jit(solution)/shard_map/reduce_scatter | solution.py:56
  214.3 1.4 fusion.29
  215.7 13.4 %psum.22 = f32[2048]{0:T(1024)S(1)} all-reduce(f32[2048]{0:T(1024)S(1)} %get-tuple-element.17), channel_id=1, replica_groups=mesh['dp'=32,'tensor'=8] {'tensor'}, use_global_device_ids=true, to_apply=%region_13.0 | all-reduce | flops 2048 | bytes 16384 | tf_op jit(solution)/shard_map/psum | solution.py:71
  229.1 137.8 %all-reduce = (f32[3,7,256]{2,0,1:T(4,128)S(1)}, f32[2048]{0:T(1024)}) all-reduce(f32[3,7,256]{2,0,1:T(4,128)S(1)} %constant_dynamic-update-slice_fusion, f32[2048]{0:T(1024)S(1)} %psum.22), channel_id=1, replica_groups=mesh['dp'=32,'tensor'=8] {'dp'}, use_global_device_ids=true, to_apply=%region_11.0 | all-reduce | flops 7424 | bytes 59392 | tf_op jit(solution)/shard_map/psum | solution.py:70
  366.8 0.6 copy.12
  367.5 2.2 fusion.23
  (24 shorter events, 0.1 us)
Async XLA Ops:
  7.2 64.9 %all-gather.5.cloned.1.call-start = ((), (), s32[]{:S(2)}) async-start(), calls=%async_computation.3 | async-start | bytes 3244032 | tf_op jit(solution)/shard_map/all_gather | solution.py:19
  7.9 119.0 %all-gather.3.cloned.1.call-start = ((), (), s32[]{:S(2)}) async-start(), calls=%async_computation.2 | async-start | bytes 4718592 | tf_op jit(solution)/shard_map/all_gather | solution.py:20
  11.2 203.0 %reduce-scatter.3.cloned.1.call-start = ((), (), s32[]{:S(2)}) async-start(), calls=%async_computation.4 | async-start | bytes 4718592 | tf_op jit(solution)/shard_map/reduce_scatter | solution.py:56
  133.5 5.5 %collective-permute-start = (bf16[6,3,256]{2,0,1:T(8,128)(2,1)S(1)}, bf16[6,3,256]{2,0,1:T(8,128)(2,1)S(1)}, u32[]{:S(2)}, u32[]{:S(2)}) collective-permute-start(bf16[6,3,256]{2,0,1:T(8,128)(2,1)S(1)} %slice.120), channel_id=1, source_target_pairs={{0,8},{8,16},{16,24},{24,32},{32,40},{40,48},{48,56},{56,64},{64,7... | collective-permute-start | bytes 27656 | tf_op jit(solution)/shard_map/ppermute | solution.py:10
  139.4 2.6 copy-start.1
  146.0 6.8 %collective-permute-start.1 = (f32[6,3,256]{2,0,1:T(8,128)S(1)}, f32[6,3,256]{2,0,1:T(8,128)S(1)}, u32[]{:S(2)}, u32[]{:S(2)}) collective-permute-start(f32[6,3,256]{2,0,1:T(8,128)S(1)} %slice.131), channel_id=1, source_target_pairs={{8,0},{16,8},{24,16},{32,24},{40,32},{48,40},{56,48},{64,56},{72,6... | collective-permute-start | bytes 55304 | tf_op jit(solution)/shard_map/ppermute | solution.py:10
  153.0 2.7 copy-start.3
  160.9 208.8 %reduce-scatter.5.cloned.1.call-start = ((), (), s32[]{:S(2)}) async-start(), calls=%async_computation.5 | async-start | bytes 3244032 | tf_op jit(solution)/shard_map/reduce_scatter | solution.py:62
  168.6 45.7 %copy-start = (bf16[128,2048]{1,0:T(8,128)(2,1)S(1)}, bf16[128,2048]{1,0:T(8,128)(2,1)}, u32[]{:S(2)}) copy-start(bf16[128,2048]{1,0:T(8,128)(2,1)} %param.5) | copy-start | bytes 1572868
  168.6 45.7 %copy-start.2 = (f32[2048]{0:T(1024)S(1)}, f32[2048]{0:T(1024)}, u32[]{:S(2)}) copy-start(f32[2048]{0:T(1024)} %param.6) | copy-start | bytes 24580
Sparse Core Ops, SparseCore 0:
  10.7 61.3 all-gather.4
  74.4 52.5 all-gather.2
  161.0 53.2 reduce-scatter.2
  218.6 92.5 reduce-scatter.4
